TPU v7x, 32 devices: a whole 2x2x4 slice. The times are simulated.
32 devices in a mesh: grp: 4 (over y, x), rows: 8 (over z, core).
Axes of the slice: x: 2, y: 2, z: 4, core: 2. Of those that a mesh axis runs over, the one named last changes fastest.
Arguments:
- stationary: bfloat16 [81920, 512], P(('grp', 'rows')), may hold values from -6 to 6
- rotor_rows: bfloat16 [1024, 512], P(('grp', 'rows')), may hold values from -6 to 6
- owners: int32 [1024, 1], P(('grp', 'rows')), may hold values from 0 to 7; in each aligned block of 32 rows (0 to 31, 32 to 63, ...) at most 6 rows name the same one
- counts: int32 [32], P(('grp', 'rows')), may hold values from 24 to 32
- omega: bfloat16 [512, 192], replicated, may hold values from -0.25 to 0.25
Outputs:
- basis_stationary: bfloat16 [81920, 192], P(('grp', 'rows'))
- basis_rotor: bfloat16 [1536, 192], P(('grp', 'rows'))
- factor: float32 [192, 192], replicated
Inputs may be any that keep to these rules, and one draw needn't show every extreme that they name: `owners`: in the rotor rows of one device no owner is named more than 6 times.
All inputs are finite; a program needn't handle non-finite values.
Results may differ from a plain program's by a relative error of at most 0.0056.
Values may be sent and summed in bfloat16 or wider, within the bound.
No kernel may reach another device: no remote copies, remote signals or barrier semaphores. Data moves between devices by JAX's collectives and lax.ppermute only.
A program may use at most 64 MiB of HBM per device.

v0:
```python
import jax
import jax.numpy as jnp
from jax import lax
from jax.sharding import PartitionSpec as P

CAP = 6


def sketch_block(block, omega):
    return jnp.dot(block, omega, preferred_element_type=jnp.float32).astype(jnp.bfloat16)


def per_device(stationary, rotor_rows, owners, counts, omega):
    n_rows = lax.axis_size("rows")
    n_grp = lax.axis_size("grp")
    rot_dev = rotor_rows.shape[0]
    stat_dev = stationary.shape[0]
    total = n_grp * n_rows * (stat_dev + rot_dev)
    targets = owners[:, 0]
    live = lax.iota(jnp.int32, rot_dev) < counts[0]
    onehot = ((targets[:, None] == lax.iota(jnp.int32, n_rows)[None, :]) & live[:, None]).astype(
        jnp.int32
    )
    rank = jnp.sum((jnp.cumsum(onehot, axis=0) - onehot) * onehot, axis=1)
    slot = jnp.where(live, targets * CAP + rank, -1)
    select = (lax.iota(jnp.int32, n_rows * CAP)[:, None] == slot[None, :]).astype(jnp.bfloat16)
    sketch_stat = sketch_block(stationary, omega)
    outgoing = jnp.dot(select, rotor_rows, preferred_element_type=jnp.float32).astype(jnp.bfloat16)
    outgoing = outgoing.reshape(n_rows, CAP, -1)
    arrived_rows = lax.all_to_all(outgoing, "rows", split_axis=0, concat_axis=0, tiled=True)
    arrived = sketch_block(arrived_rows.reshape(n_rows * CAP, -1), omega)
    local = jnp.concatenate([sketch_stat, arrived], axis=0)
    gram = (
        lax.dot_general(local, local, (((0,), (0,)), ((), ())), preferred_element_type=jnp.float32)
        / total
    )
    lower = jnp.linalg.cholesky(lax.psum(gram, ("grp", "rows")))
    solved = lax.linalg.triangular_solve(
        lower, local.astype(jnp.float32).T, left_side=True, lower=True
    )
    basis = solved.T.astype(jnp.bfloat16)
    return (basis[:stat_dev], basis[stat_dev:], lower.T)


def solution(mesh):
    return jax.shard_map(
        per_device,
        mesh=mesh,
        in_specs=(
            P(("grp", "rows"), None),
            P(("grp", "rows"), None),
            P(("grp", "rows"), None),
            P(("grp", "rows")),
            P(),
        ),
        out_specs=(P(("grp", "rows"), None), P(("grp", "rows"), None), P()),
        check_vma=False,
    )
```

profile of v0, /device:TPU:8, one launch (start us, length us, event | category | flops | bytes accessed | tf_op | source)
XLA Modules:
  0.0 226.8 jit_solution(445382293434304383)
XLA Ops:
  8.0 0.7 fusion.12
  8.8 0.8 select_reduce_fusion.2
  9.6 0.7 add_select_fusion
  10.3 0.9 convolution_convert_fusion.2
  11.8 5.3 %all-to-all-start = ((bf16[8,6,512]{2,1,0:T(8,128)(2,1)}), bf16[8,6,512]{2,1,0:T(8,128)(2,1)S(1)}, u32[]{:S(2)}, u32[]{:S(2)}) async-start(bf16[8,6,512]{2,1,0:T(8,128)(2,1)} %reshape.49), calls=%async_computation | async-start | bytes 131072 | tf_op jit(solution)/shard_map/all_to_all | solution.py:30
  17.2 2.9 %convolution_convert_fusion = bf16[2560,192]{0,1:T(8,128)(2,1)} fusion(bf16[2560,512]{1,0:T(8,128)(2,1)S(1)} %copy-done, bf16[512,192]{0,1:T(8,128)(2,1)} %param.9), kind=kOutput, calls=%fused_computation | convolution fusion | flops 503808000 | bytes 3801088 | tf_op jit(solution)/shard_map/dot_general | solution.py:10
  20.1 1.6 all-to-all-done
  22.1 2.7 %convolution_multiply_fusion = f32[192,192]{0,1:T(8,128)} fusion(bf16[48,192]{0,1:T(8,128)(2,1)S(1)} %copy.20, bf16[2560,192]{0,1:T(8,128)(2,1)} %convolution_convert_fusion), kind=kOutput, calls=%fused_computation.4 | convolution fusion | flops 194322432 | bytes 1148928 | tf_op jit(solution)/shard_map/dot_general | solution.py:34
  24.8 2.3 fusion.2
  27.1 124.5 %all-reduce.5.cloned.1.call-done = f32[192,192]{0,1:T(8,128)} async-done(((f32[192,192]{0,1:T(8,128)}), f32[192,192]{0,1:T(8,128)}) %all-reduce.5.cloned.1.call-update) | async-done | bytes 147472 | tf_op jit(solution)/shard_map/psum | solution.py:37
  151.6 1.0 copy.22
  152.6 1.0 fusion.3
  153.6 11.7 %cholesky.51 = f32[128,128]{1,0:T(8,128)S(1)} custom-call(f32[128,128]{1,0:T(8,128)S(1)} %cholesky.124), custom_call_target="Cholesky" | custom-call | tf_op jit(solution)/shard_map/jit(cholesky)/cholesky | solution.py:37
  166.0 9.8 %custom-call.14 = f32[1,128,128]{1,2,0:T(8,128)S(1)} custom-call(f32[1,128,128]{2,1,0:T(8,128)S(1)} %get-tuple-element.35), custom_call_target="InvertDiagBlocksLowerTriangular" | custom-call | tf_op jit(solution)/shard_map/jit(cholesky)/cholesky | solution.py:37
  176.2 5.8 %cholesky.110 = f32[64,64]{1,0:T(8,128)S(1)} custom-call(f32[64,64]{1,0:T(8,128)S(1)} %convolution_subtract_fusion.1), custom_call_target="Cholesky" | custom-call | tf_op jit(solution)/shard_map/jit(cholesky)/cholesky | solution.py:37
  184.7 20.3 %custom-call.15 = f32[2,128,128]{1,2,0:T(8,128)} custom-call(f32[2,128,128]{2,1,0:T(8,128)S(1)} %pad_maximum_fusion.2), custom_call_target="InvertDiagBlocksLowerTriangular" | custom-call | tf_op jit(solution)/shard_map/triangular_solve | solution.py:38
  205.0 2.0 fusion.15
  207.0 2.4 %convolution_subtract_fusion = f32[64,2608]{1,0:T(8,128)S(1)} fusion(f32[128,2608]{0,1:T(8,128)S(1)} %get-tuple-element.41, bf16[192,2608]{1,0:T(8,128)(2,1)} %fusion.2, f32[192,192]{1,0:T(8,128)} %copy-done.2), kind=kOutput, calls=%fused_computation.1 | convolution fusion | flops 256710656 | bytes 2379776 | tf_op jit(solution)/shard_map/triangular_solve | solution.py:38
  209.4 2.2 convolution_convert_fusion.1
  211.7 2.1 copy.23
  213.8 1.3 maximum_bitcast_fusion
  215.7 1.1 slice.71
  216.9 0.8 copy.25
  217.7 2.3 %copy.24 = bf16[2560,192]{0,1:T(8,128)(2,1)} copy(bf16[2560,192]{1,0:T(8,128)(2,1)} %slice.71) | data formatting | bytes 1966080
  (29 shorter events, 4.1 us)
Async XLA Ops:
  7.2 10.0 %copy-start = (bf16[2560,512]{1,0:T(8,128)(2,1)S(1)}, bf16[2560,512]{1,0:T(8,128)(2,1)}, u32[]{:S(2)}) copy-start(bf16[2560,512]{1,0:T(8,128)(2,1)} %param.5) | copy-start | bytes 7864324
  11.8 10.0 %all-to-all-start = ((bf16[8,6,512]{2,1,0:T(8,128)(2,1)}), bf16[8,6,512]{2,1,0:T(8,128)(2,1)S(1)}, u32[]{:S(2)}, u32[]{:S(2)}) async-start(bf16[8,6,512]{2,1,0:T(8,128)(2,1)} %reshape.49), calls=%async_computation | async-start | bytes 131072 | tf_op jit(solution)/shard_map/all_to_all | solution.py:30
  17.1 134.4 %all-reduce.5.cloned.1.call-start = ((), (), s32[]{:S(2)}) async-start(), calls=%async_computation.1 | async-start | bytes 393216 | tf_op jit(solution)/shard_map/psum | solution.py:37
  17.2 4.6 %copy-start.1 = (bf16[512,192]{0,1:T(8,128)(2,1)S(1)}, bf16[512,192]{0,1:T(8,128)(2,1)}, u32[]{:S(2)}) copy-start(bf16[512,192]{0,1:T(8,128)(2,1)} %param.9) | copy-start | bytes 589828
  184.1 0.7 copy-start.2
Sparse Core Ops, SparseCore 0:
  24.9 126.6 all-reduce.4
where the time goes:
time: 228 us; the launch traced here: 227 us
  waiting for transfers between devices  126 us (55%)
  other arithmetic  56 us (25%)
  between operations  16.3 us (7%)
  matrix products  13.7 us (6%)
  local copies, waits for them, and re-layouts  9.36 us (4%)
  starting transfers between devices  5.33 us (2%)
    psum x1, waiting for transfers between devices, per_device(): lower = jnp.linalg.cholesky(lax.psum(gram, ('grp', 'rows')))  125 us
    another operation x7, other arithmetic, per_device(): lower = jnp.linalg.cholesky(lax.psum(gram, ('grp', 'rows')))  28.7 us
    another operation x5, other arithmetic, per_device(): lax.linalg.triangular_solve(lower, local.astype(jnp.float32).T, left_side...  20.4 us
    another operation x3, matrix products, per_device(): lax.linalg.triangular_solve(lower, local.astype(jnp.float32).T, left_side...  6.65 us
    all_to_all x1, starting transfers between devices, per_device(): lax.all_to_all(outgoing, 'rows', split_axis=0, concat_axis=0, tiled=True)  5.32 us
  transfers between devices with their start and end apart: 2, of which 2 were waited for; matrix products, arithmetic and copies ran while one was open for 2% of the time, Pallas kernels for 0%

commit v1 on v0

--- a/solution.py
+++ b/solution.py
@@ -4,6 +4,9 @@
 from jax.sharding import PartitionSpec as P
 
 CAP = 6
+slot_make = lambda frame_in: jnp.sum(
+    jax.lax.all_gather(frame_in, axis_name=("grp", "rows")), axis=0
+)
 
 
 def sketch_block(block, omega):
@@ -34,7 +37,7 @@
         lax.dot_general(local, local, (((0,), (0,)), ((), ())), preferred_element_type=jnp.float32)
         / total
     )
-    lower = jnp.linalg.cholesky(lax.psum(gram, ("grp", "rows")))
+    lower = jnp.linalg.cholesky(slot_make(gram))
     solved = lax.linalg.triangular_solve(
         lower, local.astype(jnp.float32).T, left_side=True, lower=True
     )

time: 228 us -> 172 us (0.75)
  waiting for transfers between devices: 126 us -> 68.2 us
  other arithmetic: 56 us -> 58.3 us
    psum x1 -> x0, waiting for transfers between devices: 125 us -> none  [per_device(): lower = jnp.linalg.cholesky(lax.psum(gram, ('grp', 'rows')))]
    all_gather x0 -> x1, waiting for transfers between devices: none -> 66.5 us  [jax.lax.all_gather(frame_in, axis_name=('grp', 'rows'))]
    reduce_sum x0 -> x1, other arithmetic: none -> 3.24 us  [jnp.sum(jax.lax.all_gather(frame_in, axis_name=('grp', 'rows')), axis=0)]
  transfers between devices with their start and end apart: 2 -> 2, of which waited for: 2 -> 2; matrix products, arithmetic and copies ran while one was open for 2% -> 3% of each run, Pallas kernels for 0% -> 0%
where the time goes in v1:
time: 172 us; the launch traced here: 170 us
  waiting for transfers between devices  68.2 us (40%)
  other arithmetic  58.3 us (34%)
  between operations  16.3 us (9%)
  matrix products  13.7 us (8%)
  local copies, waits for them, and re-layouts  8.43 us (5%)
  starting transfers between devices  5.33 us (3%)
    all_gather x1, waiting for transfers between devices, jax.lax.all_gather(frame_in, axis_name=('grp', 'rows'))  66.5 us
    another operation x7, other arithmetic, per_device(): lower = jnp.linalg.cholesky(slot_make(gram))  28.7 us
    another operation x5, other arithmetic, per_device(): lax.linalg.triangular_solve(lower, local.astype(jnp.float32).T, left_side...  20.4 us
    another operation x3, matrix products, per_device(): lax.linalg.triangular_solve(lower, local.astype(jnp.float32).T, left_side...  6.64 us
    all_to_all x1, starting transfers between devices, per_device(): lax.all_to_all(outgoing, 'rows', split_axis=0, concat_axis=0, tiled=True)  5.32 us
    unnamed x8, local copies, waits for them, and re-layouts  3.68 us
  transfers between devices with their start and end apart: 2, of which 2 were waited for; matrix products, arithmetic and copies ran while one was open for 3% of the time, Pallas kernels for 0%

profile of v1, /device:TPU:8, one launch (start us, length us, event | category | flops | bytes accessed | tf_op | source)
XLA Modules:
  0.0 170.2 jit_solution(338510116373406820)
XLA Ops:
  8.0 0.7 fusion.12
  8.8 0.8 select_reduce_fusion.2
  9.6 0.7 add_select_fusion
  10.3 0.9 convolution_convert_fusion.2
  11.2 0.7 reshape.49
  11.8 5.3 %all-to-all-start = ((bf16[8,6,512]{2,1,0:T(8,128)(2,1)}), bf16[8,6,512]{2,1,0:T(8,128)(2,1)S(1)}, u32[]{:S(2)}, u32[]{:S(2)}) async-start(bf16[8,6,512]{2,1,0:T(8,128)(2,1)} %reshape.49), calls=%async_computation | async-start | bytes 131072 | tf_op jit(solution)/shard_map/all_to_all | solution.py:33
  17.2 2.9 %convolution_convert_fusion = bf16[2560,192]{0,1:T(8,128)(2,1)} fusion(bf16[2560,512]{1,0:T(8,128)(2,1)S(1)} %copy-done, bf16[512,192]{0,1:T(8,128)(2,1)} %param.9), kind=kOutput, calls=%fused_computation | convolution fusion | flops 503808000 | bytes 3801088 | tf_op jit(solution)/shard_map/dot_general | solution.py:13
  20.1 1.7 all-to-all-done
  22.1 2.7 %convolution_multiply_fusion = f32[192,192]{1,0:T(8,128)} fusion(bf16[48,192]{0,1:T(8,128)(2,1)S(1)} %copy.23, bf16[2560,192]{0,1:T(8,128)(2,1)} %convolution_convert_fusion), kind=kOutput, calls=%fused_computation.4 | convolution fusion | flops 194322432 | bytes 1148928 | tf_op jit(solution)/shard_map/dot_general | solution.py:37
  24.8 2.3 %fusion.2 = bf16[192,2608]{1,0:T(8,128)(2,1)} fusion(bf16[48,192]{0,1:T(8,128)(2,1)S(1)} %copy.23, bf16[2560,192]{0,1:T(8,128)(2,1)} %convolution_convert_fusion), kind=kLoop, calls=%fused_computation.11 | loop fusion | flops 2002944 | bytes 2002944 | tf_op jit(solution)/shard_map/transpose | solution.py:42
  27.1 66.5 %all-gather.3.cloned.1.call-done = f32[6144,192]{1,0:T(8,128)} async-done(((f32[192,192]{1,0:T(8,128)}), f32[6144,192]{1,0:T(8,128)}) %all-gather.3.cloned.1.call-update) | async-done | bytes 4718608 | tf_op jit(solution)/shard_map/all_gather | solution.py:8
  93.6 3.2 %reduce_sum.19 = f32[192,192]{1,0:T(8,128)S(1)} reduce(f32[32,192,192]{2,1,0:T(8,128)} %bitcast.44, f32[]{:T(128)} %constant.91.clone.1), dimensions={0}, to_apply=%region_2.3 | reduce | flops 1142784 | bytes 4866052 | tf_op jit(solution)/shard_map/reduce_sum | solution.py:7
  97.0 11.7 %cholesky.51 = f32[128,128]{1,0:T(8,128)S(1)} custom-call(f32[128,128]{1,0:T(8,128)S(1)} %cholesky.124), custom_call_target="Cholesky" | custom-call | tf_op jit(solution)/shard_map/jit(cholesky)/cholesky | solution.py:40
  108.7 9.8 %custom-call.14 = f32[1,128,128]{1,2,0:T(8,128)S(1)} custom-call(f32[1,128,128]{2,1,0:T(8,128)S(1)} %get-tuple-element.38), custom_call_target="InvertDiagBlocksLowerTriangular" | custom-call | tf_op jit(solution)/shard_map/jit(cholesky)/cholesky | solution.py:40
  118.9 5.8 %cholesky.110 = f32[64,64]{1,0:T(8,128)S(1)} custom-call(f32[64,64]{1,0:T(8,128)S(1)} %convolution_subtract_fusion.1), custom_call_target="Cholesky" | custom-call | tf_op jit(solution)/shard_map/jit(cholesky)/cholesky | solution.py:40
  128.1 20.3 %custom-call.15 = f32[2,128,128]{1,2,0:T(8,128)} custom-call(f32[2,128,128]{2,1,0:T(8,128)S(1)} %pad_maximum_fusion.2), custom_call_target="InvertDiagBlocksLowerTriangular" | custom-call | tf_op jit(solution)/shard_map/triangular_solve | solution.py:41
  148.4 2.0 %fusion.15 = (bf16[128,2608]{0,1:T(8,128)(2,1)S(1)}, f32[128,2608]{0,1:T(8,128)S(1)}) fusion(bf16[192,2608]{1,0:T(8,128)(2,1)} %fusion.2, f32[2,128,128]{1,2,0:T(8,128)} %custom-call.15), kind=kOutput, calls=%fused_computation.50 | convolution fusion | flops 513087488 | bytes 2756608 | tf_op jit(solution)/shard_map/triangular_solve | solution.py:41
  150.4 2.4 %convolution_subtract_fusion = f32[64,2608]{1,0:T(8,128)S(1)} fusion(f32[128,2608]{0,1:T(8,128)S(1)} %get-tuple-element.44, bf16[192,2608]{1,0:T(8,128)(2,1)} %fusion.2, f32[192,192]{1,0:T(8,128)} %copy-done.2), kind=kOutput, calls=%fused_computation.1 | convolution fusion | flops 256710656 | bytes 2379776 | tf_op jit(solution)/shard_map/triangular_solve | solution.py:41
  152.8 2.2 %convolution_convert_fusion.1 = bf16[64,2608]{1,0:T(8,128)(2,1)} fusion(f32[64,2608]{1,0:T(8,128)S(1)} %convolution_subtract_fusion, f32[2,128,128]{1,2,0:T(8,128)} %custom-call.15), kind=kOutput, calls=%fused_computation.2 | convolution fusion | flops 128355328 | bytes 1034240 | tf_op jit(solution)/shard_map/triangular_solve | solution.py:41
  155.0 2.1 %copy.25 = bf16[64,2608]{0,1:T(8,128)(2,1)} copy(bf16[64,2608]{1,0:T(8,128)(2,1)} %convolution_convert_fusion.1) | data formatting | bytes 667648 | tf_op jit(solution)/shard_map/convert.7
  157.1 1.3 maximum_bitcast_fusion
  158.5 1.1 slice.71
  160.2 2.3 %copy.26 = bf16[2560,192]{0,1:T(8,128)(2,1)} copy(bf16[2560,192]{1,0:T(8,128)(2,1)} %slice.71) | data formatting | bytes 1966080
  162.5 0.8 copy.27
  (30 shorter events, 3.6 us)
Async XLA Ops:
  7.2 10.0 %copy-start = (bf16[2560,512]{1,0:T(8,128)(2,1)S(1)}, bf16[2560,512]{1,0:T(8,128)(2,1)}, u32[]{:S(2)}) copy-start(bf16[2560,512]{1,0:T(8,128)(2,1)} %param.5) | copy-start | bytes 7864324
  11.8 10.0 %all-to-all-start = ((bf16[8,6,512]{2,1,0:T(8,128)(2,1)}), bf16[8,6,512]{2,1,0:T(8,128)(2,1)S(1)}, u32[]{:S(2)}, u32[]{:S(2)}) async-start(bf16[8,6,512]{2,1,0:T(8,128)(2,1)} %reshape.49), calls=%async_computation | async-start | bytes 131072 | tf_op jit(solution)/shard_map/all_to_all | solution.py:33
  17.1 4.7 %copy-start.1 = (bf16[512,192]{0,1:T(8,128)(2,1)S(1)}, bf16[512,192]{0,1:T(8,128)(2,1)}, u32[]{:S(2)}) copy-start(bf16[512,192]{0,1:T(8,128)(2,1)} %param.9) | copy-start | bytes 589828
  17.1 76.4 %all-gather.3.cloned.1.call-start = ((), (), s32[]{:S(2)}) async-start(), calls=%async_computation.1 | async-start | bytes 6488064 | tf_op jit(solution)/shard_map/all_gather | solution.py:8
  127.4 0.7 copy-start.2
Sparse Core Ops, SparseCore 0:
  24.9 68.5 all-gather.2
